TPU v7x, 512 devices: a whole 4x8x8 slice. The times are simulated.
512 devices in a mesh: frames: 64 (over x, y, core), tex: 8 (over z).
Axes of the slice: x: 4, y: 8, z: 8, core: 2. Of those that a mesh axis runs over, the one named last changes fastest.
Arguments:
- texture: bfloat16 [512, 16384], P('tex'), may hold values from -6 to 6
- requests: int32 [512, 32], P(('frames', 'tex')), may hold values from 0 to 63, as said below
- block_slot: int32 [512, 32], P(('frames', 'tex')), may hold values from 0 to 31
- texel_cell: int32 [512, 4096], P(('frames', 'tex')), may hold values from 0 to 960
- uv_frac: float32 [512, 2, 4096], P(('frames', 'tex')), may hold values from 0 to 1
- conv_weight: bfloat16 [32, 144], replicated, may hold values from -0.5 to 0.5
- cotangent: bfloat16 [512, 32, 4096], P(('frames', 'tex')), may hold values from -6 to 6
Outputs:
- rendered: bfloat16 [512, 32, 4096], P(('frames', 'tex'))
- texture_grad: float32 [512, 16384], P('tex', 'frames')
- weight_grad: float32 [32, 144], replicated
Inputs may be any that keep to these rules, and one draw needn't show every extreme that they name: The 4 tile numbers one renderer requests from one owner are distinct.
All inputs are finite; a program needn't handle non-finite values.
Results may differ from a plain program's by a relative error of at most 0.007.
Values may be sent and summed in bfloat16 or wider, within the bound.
No kernel may reach another device: no remote copies, remote signals or barrier semaphores. Data moves between devices by JAX's collectives and lax.ppermute only.
A program may use at most 64 MiB of HBM per device.

v0:
```python
import math
import jax
import jax.numpy as jnp
from jax import lax
from jax.sharding import PartitionSpec as P

CH = 16


def taps_and_weights(cell_row, frac_row, side):
    column = cell_row % (side - 1)
    row_index = cell_row // (side - 1)
    corner = row_index * side + column
    texel_taps = jnp.stack([corner, corner + 1, corner + side, corner + side + 1])
    frac_x = frac_row[0]
    frac_y = frac_row[1]
    weights = jnp.stack(
        [
            (1.0 - frac_x) * (1.0 - frac_y),
            frac_x * (1.0 - frac_y),
            (1.0 - frac_x) * frac_y,
            frac_x * frac_y,
        ]
    )
    return (texel_taps, weights)


def sample_matrix(texel_taps, weights, texel):
    positions = lax.broadcasted_iota(jnp.int32, (texel_taps.shape[1], texel), 1)
    matrix = jnp.zeros((texel_taps.shape[1], texel), jnp.float32)
    for number in range(4):
        matrix = matrix + jnp.where(
            texel_taps[number][:, None] == positions, weights[number][:, None], jnp.float32(0.0)
        )
    return matrix.astype(jnp.bfloat16)


def shifted(picture, shift_y, shift_x):
    height = picture.shape[1]
    width = picture.shape[2]
    padded_input = jnp.pad(picture, ((0, 0), (1, 1), (1, 1)))
    return padded_input[:, 1 + shift_y : 1 + shift_y + height, 1 + shift_x : 1 + shift_x + width]


def render_one(fetched, slot_row, cell_row, frac_row, conv_weight, cot_row):
    visible = fetched.shape[0]
    channels = fetched.shape[1]
    texel = fetched.shape[2]
    side = math.isqrt(texel)
    height = slot_row.shape[0]
    width = cell_row.shape[0] // height
    group_size = math.gcd(height, 16)
    group_count = height // group_size
    texel_taps, weights = taps_and_weights(cell_row, frac_row, side)
    taps_grouped = texel_taps.reshape(4, group_count, group_size * width).transpose(1, 0, 2)
    weights_grouped = weights.reshape(4, group_count, group_size * width).transpose(1, 0, 2)
    slots_grouped = slot_row.reshape(group_count, group_size)

    def forward(inputs):
        taps_part, weights_part, slots_part = inputs
        texture_lookup = sample_matrix(taps_part, weights_part, texel).reshape(
            group_size, width, texel
        )
        selected_entries = jnp.take(fetched, slots_part, axis=0)
        feature_maps = jnp.einsum(
            "qfm,qzm->qfz", selected_entries, texture_lookup, preferred_element_type=jnp.float32
        )
        return feature_maps.astype(jnp.bfloat16)

    grouped_features = lax.map(forward, (taps_grouped, weights_grouped, slots_grouped))
    feature_maps = grouped_features.transpose(2, 0, 1, 3).reshape(channels, height, width)
    offsets = [(shift_y, shift_x) for shift_y in (-1, 0, 1) for shift_x in (-1, 0, 1)]
    columns = jnp.concatenate(
        [shifted(feature_maps, shift_y, shift_x) for shift_y, shift_x in offsets], axis=0
    )
    columns = columns.reshape(9 * channels, height * width)
    preact = jnp.dot(conv_weight, columns, preferred_element_type=jnp.float32)
    sigmoid_pre = jax.nn.sigmoid(preact)
    rendered = (preact * sigmoid_pre).astype(jnp.bfloat16)
    pre_grad = (
        cot_row.astype(jnp.float32) * sigmoid_pre * (1.0 + preact * (1.0 - sigmoid_pre))
    ).astype(jnp.bfloat16)
    weight_local = jnp.einsum("op,kp->ok", pre_grad, columns, preferred_element_type=jnp.float32)
    col_grad = jnp.einsum("ok,op->kp", conv_weight, pre_grad, preferred_element_type=jnp.float32)
    col_grad = col_grad.reshape(9, channels, height, width)
    feat_grad = jnp.zeros((channels, height, width), jnp.float32)
    for number in range(9):
        shift_y, shift_x = offsets[number]
        feat_grad = feat_grad + shifted(col_grad[number], -shift_y, -shift_x)
    feat_grad = feat_grad.astype(jnp.bfloat16)
    grad_grouped = feat_grad.reshape(channels, group_count, group_size, width).transpose(1, 2, 0, 3)
    slot_numbers = jnp.arange(visible, dtype=jnp.int32)

    def backward(totals, inputs):
        taps_part, weights_part, slots_part, gradient_portion = inputs
        texture_lookup = sample_matrix(taps_part, weights_part, texel).reshape(
            group_size, width, texel
        )
        texel_gradient = jnp.einsum(
            "rzs,rsu->rzu", gradient_portion, texture_lookup, preferred_element_type=jnp.float32
        )
        selector = (slots_part[:, None] == slot_numbers[None, :]).astype(jnp.float32)
        added = jnp.einsum("gv,gct->vct", selector, texel_gradient, precision=lax.Precision.HIGHEST)
        return (totals + added, None)

    start = jnp.zeros((visible, channels, texel), jnp.float32)
    slot_grad, unused = lax.scan(
        backward, start, (taps_grouped, weights_grouped, slots_grouped, grad_grouped)
    )
    return (rendered, slot_grad.reshape(visible, channels * texel), weight_local)


def per_device(texture, requests, block_slot, texel_cell, uv_frac, conv_weight, cotangent):
    owners = lax.axis_size("tex")
    frame_count = lax.axis_size("frames")
    tile_count = texture.shape[0]
    tile_width = texture.shape[1]
    wanted_ids = requests.reshape(owners, -1)
    wanted = lax.all_to_all(wanted_ids, "tex", split_axis=0, concat_axis=0, tiled=True)
    served = jnp.take(texture, wanted.reshape(-1), axis=0).reshape(
        wanted.shape[0], wanted.shape[1], tile_width
    )
    returned_tiles = lax.all_to_all(served, "tex", split_axis=0, concat_axis=0, tiled=True)
    fetched = returned_tiles
    per_owner = fetched.shape[1]
    visible = owners * per_owner
    fetched = fetched.reshape(visible, CH, tile_width // CH)
    rendered, slot_grad, weight_local = render_one(
        fetched, block_slot[0], texel_cell[0], uv_frac[0], conv_weight, cotangent[0]
    )
    tile_numbers = jnp.arange(tile_count, dtype=jnp.int32)
    returned = lax.all_to_all(
        slot_grad.reshape(owners, per_owner, tile_width),
        "tex",
        split_axis=0,
        concat_axis=0,
        tiled=True,
    )
    returned_rows = returned.reshape(visible, tile_width)
    owned_flat = wanted.reshape(-1)
    selector = (tile_numbers[:, None] == owned_flat[None, :]).astype(jnp.float32)
    pool_grad = jnp.dot(selector, returned_rows, precision=lax.Precision.HIGHEST)
    texture_grad = lax.psum_scatter(pool_grad, "frames", scatter_dimension=1, tiled=True)
    norm_scale = 1.0 / math.sqrt(frame_count * owners * cotangent.shape[2])
    weight_grad = lax.psum(weight_local, ("frames", "tex")) * norm_scale
    return (rendered[None], texture_grad, weight_grad)


def solution(mesh):
    placed = (
        P("tex", None),
        P(("frames", "tex"), None),
        P(("frames", "tex"), None),
        P(("frames", "tex"), None),
        P(("frames", "tex"), None, None),
        P(),
        P(("frames", "tex"), None, None),
    )
    return jax.shard_map(
        per_device,
        mesh=mesh,
        in_specs=placed,
        out_specs=(P(("frames", "tex"), None, None), P("tex", "frames"), P()),
        check_vma=False,
    )
```

profile of v0, /device:TPU:16, one launch (start us, length us, event | category | flops | bytes accessed | tf_op | source)
XLA Modules:
  0.0 336.7 jit_solution(9305829083828627682)
XLA Ops:
  9.8 10.3 %all-to-all-start = ((s32[8,1,4]{2,1,0:T(1,128)}), s32[8,1,4]{2,1,0:T(1,128)S(1)}, u32[]{:S(2)}, u32[]{:S(2)}) async-start(s32[8,1,4]{2,1,0:T(1,128)} %bitcast.12), calls=%async_computation | async-start | bytes 8192 | tf_op jit(solution)/shard_map/all_to_all | solution.py:119
  21.0 6.8 %all-to-all-done = s32[8,1,4]{2,1,0:T(1,128)S(1)} async-done(((s32[8,1,4]{2,1,0:T(1,128)}), s32[8,1,4]{2,1,0:T(1,128)S(1)}, u32[]{:S(2)}, u32[]{:S(2)}) %all-to-all-start) | async-done | bytes 160 | tf_op jit(solution)/shard_map/all_to_all | solution.py:119
  31.1 2.7 broadcast_select_fusion
  33.9 3.6 %all-to-all-start.1 = ((bf16[8,4,16384]{2,1,0:T(4,128)(2,1)}), bf16[8,4,16384]{2,1,0:T(4,128)(2,1)S(1)}, u32[]{:S(2)}, u32[]{:S(2)}) async-start(bf16[8,4,16384]{2,1,0:T(4,128)(2,1)} %broadcast_select_fusion), calls=%async_computation.1 | async-start | bytes 2097152 | tf_op jit(solution)/shard_map/all_to_all | solution.py:123
  38.5 26.4 %all-to-all-done.1 = bf16[8,4,16384]{2,1,0:T(4,128)(2,1)S(1)} async-done(((bf16[8,4,16384]{2,1,0:T(4,128)(2,1)}), bf16[8,4,16384]{2,1,0:T(4,128)(2,1)S(1)}, u32[]{:S(2)}, u32[]{:S(2)}) %all-to-all-start.1) | async-done | bytes 1048608 | tf_op jit(solution)/shard_map/all_to_all | solution.py:123
  64.9 1.6 reshape.367
  66.5 16.0 %while.21 = (s32[]{:T(128)}, bf16[2,16,16,128]{3,2,1,0:T(8,128)(2,1)S(1)}, s32[2,16]{1,0:T(2,128)S(1)}, bf16[32,16,1024]{2,1,0:T(8,128)(2,1)}, s32[2,4,2048]{2,1...) while((s32[]{:T(128)}, ...), condition=%wide.region_1.2_spmd, body=%wide.region_0.1_spmd.sunk | while | flops 92570768 | bytes 1840149 | solution.py:70
  66.7 1.8 gather_fusion
  68.5 6.1 %fusion.58 = bf16[2,16,16,128]{3,2,1,0:T(8,128)(2,1)S(1)} fusion(bf16[2,16,16,128]{3,2,1,0:T(8,128)(2,1)S(1)} %get-tuple-element.284, s32[]{:T(128)S(6)} %copy.61, f32[16,128]{1,0:T(8,128)S(1)} %bitcast.200, s32[16,128]{1,0:T(8,128)S(1)} %bitcast.204, f32[16,128]{1,0:T(8,128)S(1)} %bitcast.198, s32[16,128]{1,0:T(8,128)S(1)} %bitcast.202, ...), kind=kOutput, calls=%fused_computation.11.clone.1 | convolution fusion | flops 92569600 | bytes 655876 | tf_op jit(solution)/shard_map/while/body/eval_jaxpr/qfm,qzm->qfz/dot_general | solution.py:65
  74.7 1.8 gather_fusion
  76.5 6.1 %fusion.58 = bf16[2,16,16,128]{3,2,1,0:T(8,128)(2,1)S(1)} fusion(bf16[2,16,16,128]{3,2,1,0:T(8,128)(2,1)S(1)} %get-tuple-element.284, s32[]{:T(128)S(6)} %copy.61, f32[16,128]{1,0:T(8,128)S(1)} %bitcast.200, s32[16,128]{1,0:T(8,128)S(1)} %bitcast.204, f32[16,128]{1,0:T(8,128)S(1)} %bitcast.198, s32[16,128]{1,0:T(8,128)S(1)} %bitcast.202, ...), kind=kOutput, calls=%fused_computation.11.clone.1 | convolution fusion | flops 92569600 | bytes 655876 | tf_op jit(solution)/shard_map/while/body/eval_jaxpr/qfm,qzm->qfz/dot_general | solution.py:65
  86.4 22.6 %while.22 = (s32[]{:T(128)}, f32[32,16,1024]{2,0,1:T(8,128)}, s32[2,16]{1,0:T(2,128)S(1)}, bf16[2,16,16,128]{3,2,1,0:T(8,128)(2,1)S(1)}, s32[2,4,2048]{2,1,0:T(4...) while((s32[]{:T(128)}, f32[32,16,1024]{2,0,1:T(8,128)}, ...), condition=%wide.region_3.4_spmd.clone, body=%wide.region_2.3_spmd.clone.sunk | while | flops 193987072 | bytes 23331268 | solution.py:107
  86.6 7.3 %fusion.62 = f32[16,16,1024]{2,1,0:T(8,128)S(1)} fusion(f32[16,128]{1,0:T(8,128)S(1)} %bitcast.208, s32[16,128]{1,0:T(8,128)S(1)} %bitcast.212, f32[16,128]{1,0:T(8,128)S(1)} %bitcast.206, s32[16,128]{1,0:T(8,128)S(1)} %bitcast.210, f32[16,128]{1,0:T(8,128)S(1)} %bitcast.207, s32[16,128]{1,0:T(8,128)S(1)} %bitcast.211, f32[16,128]{1,0:T(8,128)S(1)} %bitcast.205, ...), kind=kOutput, calls=%fused_computation.36.clone.1 | convolution fusion | flops 92274688 | bytes 1179652 | tf_op jit(solution)/shard_map/while/body/eval_jaxpr/rzs,rsu->rzu/dot_general | solution.py:99
  93.8 2.6 select_add_fusion.2
  97.9 7.3 %fusion.62 = f32[16,16,1024]{2,1,0:T(8,128)S(1)} fusion(f32[16,128]{1,0:T(8,128)S(1)} %bitcast.208, s32[16,128]{1,0:T(8,128)S(1)} %bitcast.212, f32[16,128]{1,0:T(8,128)S(1)} %bitcast.206, s32[16,128]{1,0:T(8,128)S(1)} %bitcast.210, f32[16,128]{1,0:T(8,128)S(1)} %bitcast.207, s32[16,128]{1,0:T(8,128)S(1)} %bitcast.211, f32[16,128]{1,0:T(8,128)S(1)} %bitcast.205, ...), kind=kOutput, calls=%fused_computation.36.clone.1 | convolution fusion | flops 92274688 | bytes 1179652 | tf_op jit(solution)/shard_map/while/body/eval_jaxpr/rzs,rsu->rzu/dot_general | solution.py:99
  105.1 2.6 select_add_fusion.2
  109.0 4.1 %copy.26 = f32[32,16,1024]{2,1,0:T(8,128)} copy(f32[32,16,1024]{2,0,1:T(8,128)} %get-tuple-element.73) | data formatting | bytes 4194304 | tf_op jit(solution)/shard_map/while | solution.py:107
  113.2 3.7 %reshape_reshape.3 = f32[8,4,16384]{2,1,0:T(4,128)} reshape(f32[32,16,1024]{2,1,0:T(8,128)} %copy.26) | data formatting | bytes 4194304 | tf_op jit(solution)/shard_map/reshape;reshape | solution.py:133
  116.9 4.3 %all-to-all-start.2 = ((f32[8,4,16384]{2,1,0:T(4,128)}), f32[8,4,16384]{2,1,0:T(4,128)}, u32[]{:S(2)}, u32[]{:S(2)}) async-start(f32[8,4,16384]{2,1,0:T(4,128)} %reshape_reshape.3), calls=%async_computation.2 | async-start | bytes 4194304 | tf_op jit(solution)/shard_map/all_to_all | solution.py:132
  121.5 51.3 %all-to-all-done.2 = f32[8,4,16384]{2,1,0:T(4,128)} async-done(((f32[8,4,16384]{2,1,0:T(4,128)}), f32[8,4,16384]{2,1,0:T(4,128)}, u32[]{:S(2)}, u32[]{:S(2)}) %all-to-all-start.2) | async-done | bytes 2097184 | tf_op jit(solution)/shard_map/all_to_all | solution.py:132
  172.8 3.0 reshape.371
  175.8 5.4 %fusion.34 = f32[64,16384]{1,0:T(8,128)} fusion(f32[32,16384]{1,0:T(8,128)} %reshape.371, s32[32]{0:T(128)S(1)} %reshape.369), kind=kOutput, calls=%fused_computation.113 | convolution fusion | flops 402655232 | bytes 6291584 | tf_op jit(solution)/shard_map/dot_general | solution.py:142
  183.6 96.0 %psum.7 = f32[32,144]{1,0:T(8,128)S(1)} all-reduce(f32[32,144]{1,0:T(8,128)} %fusion.40), channel_id=1, replica_groups=mesh['frames'=64,'tex'=8] {'frames','tex'}, use_global_device_ids=true, to_apply=%region_5.6 | all-reduce | flops 4608 | bytes 36864 | tf_op jit(solution)/shard_map/psum | solution.py:145
  280.1 49.7 %reduce-scatter.2.cloned.1.call-done = f32[64,256]{1,0:T(8,128)} async-done(((f32[64,16384]{1,0:T(8,128)}), f32[64,256]{1,0:T(8,128)}) %reduce-scatter.2.cloned.1.call-update) | async-done | bytes 65552 | tf_op jit(solution)/shard_map/reduce_scatter | solution.py:143
  (91 shorter events, 17.9 us)
Async XLA Ops:
  7.2 21.5 %copy-start = (bf16[64,16384]{1,0:T(8,128)(2,1)S(1)}, bf16[64,16384]{1,0:T(8,128)(2,1)}, u32[]{:S(2)}) copy-start(bf16[64,16384]{1,0:T(8,128)(2,1)} %param.11) | copy-start | bytes 6291460
  9.8 17.9 %all-to-all-start = ((s32[8,1,4]{2,1,0:T(1,128)}), s32[8,1,4]{2,1,0:T(1,128)S(1)}, u32[]{:S(2)}, u32[]{:S(2)}) async-start(s32[8,1,4]{2,1,0:T(1,128)} %bitcast.12), calls=%async_computation | async-start | bytes 8192 | tf_op jit(solution)/shard_map/all_to_all | solution.py:119
  31.1 6.4 %copy-start.8 = (s32[1,32]{1,0:T(1,128)S(1)}, s32[1,32]{1,0:T(1,128)}, u32[]{:S(2)}) copy-start(s32[1,32]{1,0:T(1,128)} %param.13) | copy-start | bytes 388
  31.1 7.2 %copy-start.5 = (f32[1,2,4096]{2,1,0:T(2,128)S(1)}, f32[1,2,4096]{2,1,0:T(2,128)}, u32[]{:S(2)}) copy-start(f32[1,2,4096]{2,1,0:T(2,128)} %param.15) | copy-start | bytes 98308
  33.9 31.1 %all-to-all-start.1 = ((bf16[8,4,16384]{2,1,0:T(4,128)(2,1)}), bf16[8,4,16384]{2,1,0:T(4,128)(2,1)S(1)}, u32[]{:S(2)}, u32[]{:S(2)}) async-start(bf16[8,4,16384]{2,1,0:T(4,128)(2,1)} %broadcast_select_fusion), calls=%async_computation.1 | async-start | bytes 2097152 | tf_op jit(solution)/shard_map/all_to_all | solution.py:123
  82.5 0.9 copy-start.6
  82.5 1.0 copy-start.7
  83.5 1.1 copy-start.3
  86.6 7.3 %copy-start.1 = (f32[32,16,1024]{2,0,1:T(8,128)S(1)}, f32[32,16,1024]{2,0,1:T(8,128)}, u32[]{:S(2)}) copy-start(f32[32,16,1024]{2,0,1:T(8,128)} %get-tuple-element.317) | copy-start | bytes 6291460 | tf_op jit(solution)/shard_map/while
  96.4 1.3 copy-start.2
  97.9 7.3 %copy-start.1 = (f32[32,16,1024]{2,0,1:T(8,128)S(1)}, f32[32,16,1024]{2,0,1:T(8,128)}, u32[]{:S(2)}) copy-start(f32[32,16,1024]{2,0,1:T(8,128)} %get-tuple-element.317) | copy-start | bytes 6291460 | tf_op jit(solution)/shard_map/while
  107.7 1.3 copy-start.2
  116.9 56.0 %all-to-all-start.2 = ((f32[8,4,16384]{2,1,0:T(4,128)}), f32[8,4,16384]{2,1,0:T(4,128)}, u32[]{:S(2)}, u32[]{:S(2)}) async-start(f32[8,4,16384]{2,1,0:T(4,128)} %reshape_reshape.3), calls=%async_computation.2 | async-start | bytes 4194304 | tf_op jit(solution)/shard_map/all_to_all | solution.py:132
  121.2 208.7 %reduce-scatter.2.cloned.1.call-start = ((), (), s32[]{:S(2)}) async-start(), calls=%async_computation.4 | async-start | bytes 4259840 | tf_op jit(solution)/shard_map/reduce_scatter | solution.py:143
  181.2 1.3 copy-start.4
Sparse Core Ops, SparseCore 0:
  181.3 148.5 reduce-scatter.1
where the time goes:
time: 337 us
  waiting for transfers between devices  134 us (40%)
  blocking collectives  96 us (28%)
  matrix products  39.9 us (12%)
  local copies, waits for them, and re-layouts  25.9 us (8%)
  starting transfers between devices  18.4 us (5%)
  between operations  14.3 us (4%)
  other arithmetic  7.73 us (2%)
    psum x1, blocking collectives, per_device(): weight_grad = lax.psum(weight_local, ('frames', 'tex')) * norm_scale  96 us
    all_to_all x1, waiting for transfers between devices, per_device(): lax.all_to_all(slot_grad.reshape(owners, per_owner, tile_width), 'tex', s...  51.3 us
    reduce_scatter x1, waiting for transfers between devices, per_device(): lax.psum_scatter(pool_grad, 'frames', scatter_dimension=1, tiled=True)  49.7 us
    all_to_all x1, waiting for transfers between devices, per_device(): lax.all_to_all(served, 'tex', split_axis=0, concat_axis=0, tiled=True)  26.4 us
    dot_general x2, matrix products, backward(): jnp.einsum('rzs,rsu->rzu', gradient_portion, texture_lookup, preferred_el...  14.5 us
    dot_general x2, matrix products, forward(): jnp.einsum('qfm,qzm->qfz', selected_entries, texture_lookup, preferred_el...  12.1 us
    all_to_all x1, starting transfers between devices, per_device(): lax.all_to_all(wanted_ids, 'tex', split_axis=0, concat_axis=0, tiled=True)  10.3 us
    all_to_all x1, waiting for transfers between devices, per_device(): lax.all_to_all(wanted_ids, 'tex', split_axis=0, concat_axis=0, tiled=True)  6.76 us
  transfers between devices with their start and end apart: 4, of which 4 were waited for; matrix products, arithmetic and copies ran while one was open for 1% of the time, Pallas kernels for 0%

commit v1 on v0

--- a/solution.py
+++ b/solution.py
@@ -142,7 +142,7 @@
     pool_grad = jnp.dot(selector, returned_rows, precision=lax.Precision.HIGHEST)
     texture_grad = lax.psum_scatter(pool_grad, "frames", scatter_dimension=1, tiled=True)
     norm_scale = 1.0 / math.sqrt(frame_count * owners * cotangent.shape[2])
-    weight_grad = lax.psum(weight_local, ("frames", "tex")) * norm_scale
+    weight_grad = jnp.sum(lax.all_gather(weight_local, ("frames", "tex")), axis=0) * norm_scale
     return (rendered[None], texture_grad, weight_grad)
 
 

time: 337 us -> 346 us (1.027)
  waiting for transfers between devices: 134 us -> 232 us
  blocking collectives: 96 us -> 0 us
  other arithmetic: 7.73 us -> 14.7 us
  local copies, waits for them, and re-layouts: 25.9 us -> 22 us
    psum x1 -> x0, blocking collectives: 96 us -> none  [per_device(): weight_grad = lax.psum(weight_local, ('frames', 'tex')) * norm_scale]
    reduce_scatter x1, waiting for transfers between devices: 49.7 us -> 99.2 us  [per_device(): lax.psum_scatter(pool_grad, 'frames', scatter_dimension=1, tiled=True)]
    all_gather x0 -> x1, waiting for transfers between devices: none -> 41.8 us  [per_device(): lax.all_gather(weight_local, ('frames', 'tex'))]
    reduce_sum x0 -> x1, other arithmetic: none -> 6.98 us  [per_device(): jnp.sum(lax.all_gather(weight_local, ('frames', 'tex')), axis=0)]
    all_to_all x1, waiting for transfers between devices: 51.3 us -> 58.1 us  [per_device(): lax.all_to_all(slot_grad.reshape(owners, per_owner, tile_width), 'tex', s...]
  transfers between devices with their start and end apart: 4 -> 5, of which waited for: 4 -> 5; matrix products, arithmetic and copies ran while one was open for 1% -> 14% of each run, Pallas kernels for 0% -> 0%
where the time goes in v1:
time: 346 us
  waiting for transfers between devices  232 us (67%)
  matrix products  42.2 us (12%)
  local copies, waits for them, and re-layouts  22 us (6%)
  starting transfers between devices  18.5 us (5%)
  between operations  15.8 us (5%)
  other arithmetic  14.7 us (4%)
    reduce_scatter x1, waiting for transfers between devices, per_device(): lax.psum_scatter(pool_grad, 'frames', scatter_dimension=1, tiled=True)  99.2 us
    all_to_all x1, waiting for transfers between devices, per_device(): lax.all_to_all(slot_grad.reshape(owners, per_owner, tile_width), 'tex', s...  58.1 us
    all_gather x1, waiting for transfers between devices, per_device(): lax.all_gather(weight_local, ('frames', 'tex'))  41.8 us
    all_to_all x1, waiting for transfers between devices, per_device(): lax.all_to_all(served, 'tex', split_axis=0, concat_axis=0, tiled=True)  26.4 us
    dot_general x2, matrix products, backward(): jnp.einsum('rzs,rsu->rzu', gradient_portion, texture_lookup, preferred_el...  14.5 us
    dot_general x2, matrix products, forward(): jnp.einsum('qfm,qzm->qfz', selected_entries, texture_lookup, preferred_el...  12.1 us
    all_to_all x1, starting transfers between devices, per_device(): lax.all_to_all(wanted_ids, 'tex', split_axis=0, concat_axis=0, tiled=True)  10.3 us
    dot_general x2, matrix products, backward(): jnp.einsum('gv,gct->vct', selector, texel_gradient, precision=lax.Precisi...  7.47 us
  transfers between devices with their start and end apart: 5, of which 5 were waited for; matrix products, arithmetic and copies ran while one was open for 14% of the time, Pallas kernels for 0%

profile of v1, /device:TPU:16, one launch (start us, length us, event | category | flops | bytes accessed | tf_op | source)
XLA Modules:
  0.0 345.6 jit_solution(600318049057037819)
XLA Ops:
  10.6 10.3 %all-to-all-start = ((s32[8,1,4]{2,1,0:T(1,128)}), s32[8,1,4]{2,1,0:T(1,128)S(1)}, u32[]{:S(2)}, u32[]{:S(2)}) async-start(s32[8,1,4]{2,1,0:T(1,128)} %bitcast.12), calls=%async_computation | async-start | bytes 8192 | tf_op jit(solution)/shard_map/all_to_all | solution.py:119
  21.8 6.8 %all-to-all-done = s32[8,1,4]{2,1,0:T(1,128)S(1)} async-done(((s32[8,1,4]{2,1,0:T(1,128)}), s32[8,1,4]{2,1,0:T(1,128)S(1)}, u32[]{:S(2)}, u32[]{:S(2)}) %all-to-all-start) | async-done | bytes 160 | tf_op jit(solution)/shard_map/all_to_all | solution.py:119
  32.0 2.7 broadcast_select_fusion
  34.7 3.6 %all-to-all-start.1 = ((bf16[8,4,16384]{2,1,0:T(4,128)(2,1)}), bf16[8,4,16384]{2,1,0:T(4,128)(2,1)S(1)}, u32[]{:S(2)}, u32[]{:S(2)}) async-start(bf16[8,4,16384]{2,1,0:T(4,128)(2,1)} %broadcast_select_fusion), calls=%async_computation.1 | async-start | bytes 2097152 | tf_op jit(solution)/shard_map/all_to_all | solution.py:123
  39.4 26.4 %all-to-all-done.1 = bf16[8,4,16384]{2,1,0:T(4,128)(2,1)S(1)} async-done(((bf16[8,4,16384]{2,1,0:T(4,128)(2,1)}), bf16[8,4,16384]{2,1,0:T(4,128)(2,1)S(1)}, u32[]{:S(2)}, u32[]{:S(2)}) %all-to-all-start.1) | async-done | bytes 1048608 | tf_op jit(solution)/shard_map/all_to_all | solution.py:123
  67.4 16.0 %while.21 = (s32[]{:T(128)}, bf16[2,16,16,128]{3,2,1,0:T(8,128)(2,1)S(1)}, s32[2,16]{1,0:T(2,128)S(1)}, bf16[32,16,1024]{2,1,0:T(8,128)(2,1)}, s32[2,4,2048]{2,1...) while((s32[]{:T(128)}, ...), condition=%wide.region_1.2_spmd, body=%wide.region_0.1_spmd.sunk | while | flops 92570768 | bytes 1840149 | solution.py:70
  67.5 1.8 gather_fusion
  69.3 6.1 %fusion.58 = bf16[2,16,16,128]{3,2,1,0:T(8,128)(2,1)S(1)} fusion(bf16[2,16,16,128]{3,2,1,0:T(8,128)(2,1)S(1)} %get-tuple-element.284, s32[]{:T(128)S(6)} %copy.61, f32[16,128]{1,0:T(8,128)S(1)} %bitcast.202, s32[16,128]{1,0:T(8,128)S(1)} %bitcast.206, f32[16,128]{1,0:T(8,128)S(1)} %bitcast.200, s32[16,128]{1,0:T(8,128)S(1)} %bitcast.204, ...), kind=kOutput, calls=%fused_computation.11.clone.1 | convolution fusion | flops 92569600 | bytes 655876 | tf_op jit(solution)/shard_map/while/body/eval_jaxpr/qfm,qzm->qfz/dot_general | solution.py:65
  75.5 1.8 gather_fusion
  77.3 6.1 %fusion.58 = bf16[2,16,16,128]{3,2,1,0:T(8,128)(2,1)S(1)} fusion(bf16[2,16,16,128]{3,2,1,0:T(8,128)(2,1)S(1)} %get-tuple-element.284, s32[]{:T(128)S(6)} %copy.61, f32[16,128]{1,0:T(8,128)S(1)} %bitcast.202, s32[16,128]{1,0:T(8,128)S(1)} %bitcast.206, f32[16,128]{1,0:T(8,128)S(1)} %bitcast.200, s32[16,128]{1,0:T(8,128)S(1)} %bitcast.204, ...), kind=kOutput, calls=%fused_computation.11.clone.1 | convolution fusion | flops 92569600 | bytes 655876 | tf_op jit(solution)/shard_map/while/body/eval_jaxpr/qfm,qzm->qfz/dot_general | solution.py:65
  88.4 22.2 %while.22 = (s32[]{:T(128)}, f32[32,16,1024]{2,0,1:T(8,128)}, s32[2,16]{1,0:T(2,128)S(1)}, bf16[2,16,16,128]{3,2,1,0:T(8,128)(2,1)S(1)}, s32[2,4,2048]{2,1,0:T(4...) while((s32[]{:T(128)}, f32[32,16,1024]{2,0,1:T(8,128)}, ...), condition=%wide.region_3.4_spmd.clone, body=%wide.region_2.3_spmd.clone.sunk | while | flops 193987072 | bytes 6553995 | solution.py:107
  88.5 7.3 %fusion.62 = f32[16,16,1024]{2,1,0:T(8,128)S(1)} fusion(f32[16,128]{1,0:T(8,128)S(1)} %bitcast.210, s32[16,128]{1,0:T(8,128)S(1)} %bitcast.214, f32[16,128]{1,0:T(8,128)S(1)} %bitcast.208, s32[16,128]{1,0:T(8,128)S(1)} %bitcast.212, f32[16,128]{1,0:T(8,128)S(1)} %bitcast.209, s32[16,128]{1,0:T(8,128)S(1)} %bitcast.213, f32[16,128]{1,0:T(8,128)S(1)} %bitcast.207, ...), kind=kOutput, calls=%fused_computation.36.clone.1 | convolution fusion | flops 92274688 | bytes 1179652 | tf_op jit(solution)/shard_map/while/body/eval_jaxpr/rzs,rsu->rzu/dot_general | solution.py:99
  95.8 2.9 select_add_fusion.2
  98.8 7.3 %fusion.62 = f32[16,16,1024]{2,1,0:T(8,128)S(1)} fusion(f32[16,128]{1,0:T(8,128)S(1)} %bitcast.210, s32[16,128]{1,0:T(8,128)S(1)} %bitcast.214, f32[16,128]{1,0:T(8,128)S(1)} %bitcast.208, s32[16,128]{1,0:T(8,128)S(1)} %bitcast.212, f32[16,128]{1,0:T(8,128)S(1)} %bitcast.209, s32[16,128]{1,0:T(8,128)S(1)} %bitcast.213, f32[16,128]{1,0:T(8,128)S(1)} %bitcast.207, ...), kind=kOutput, calls=%fused_computation.36.clone.1 | convolution fusion | flops 92274688 | bytes 1179652 | tf_op jit(solution)/shard_map/while/body/eval_jaxpr/rzs,rsu->rzu/dot_general | solution.py:99
  106.1 4.5 %select_add_fusion.2 = f32[32,16,1024]{2,0,1:T(8,128)} fusion(f32[32,16,1024]{2,0,1:T(8,128)} %get-tuple-element.317, f32[16,16,1024]{2,1,0:T(8,128)S(1)} %fusion.62, pred[]{:T(512)S(6)} %compare.12, s32[16]{0:T(128)S(1)} %fusion.63), kind=kOutput, calls=%fused_computation.37.clone.1 | convolution fusion | flops 101712384 | bytes 5242945 | tf_op jit(solution)/shard_map/while/body/eval_jaxpr/gv,gct->vct/dot_general | solution.py:103
  110.6 4.1 %copy.26 = f32[32,16,1024]{2,1,0:T(8,128)} copy(f32[32,16,1024]{2,0,1:T(8,128)} %get-tuple-element.73) | data formatting | bytes 4194304 | tf_op jit(solution)/shard_map/while | solution.py:107
  114.8 3.7 %reshape_reshape.3 = f32[8,4,16384]{2,1,0:T(4,128)} reshape(f32[32,16,1024]{2,1,0:T(8,128)} %copy.26) | data formatting | bytes 4194304 | tf_op jit(solution)/shard_map/reshape;reshape | solution.py:133
  118.4 4.3 %all-to-all-start.2 = ((f32[8,4,16384]{2,1,0:T(4,128)}), f32[8,4,16384]{2,1,0:T(4,128)}, u32[]{:S(2)}, u32[]{:S(2)}) async-start(f32[8,4,16384]{2,1,0:T(4,128)} %reshape_reshape.3), calls=%async_computation.2 | async-start | bytes 4194304 | tf_op jit(solution)/shard_map/all_to_all | solution.py:132
  123.1 58.1 %all-to-all-done.2 = f32[8,4,16384]{2,1,0:T(4,128)} async-done(((f32[8,4,16384]{2,1,0:T(4,128)}), f32[8,4,16384]{2,1,0:T(4,128)}, u32[]{:S(2)}, u32[]{:S(2)}) %all-to-all-start.2) | async-done | bytes 2097184 | tf_op jit(solution)/shard_map/all_to_all | solution.py:132
  181.2 3.0 reshape.371
  184.2 5.4 %fusion.34 = f32[64,16384]{1,0:T(8,128)} fusion(f32[32,16384]{1,0:T(8,128)} %reshape.371, s32[32]{0:T(128)S(1)} %reshape.369), kind=kOutput, calls=%fused_computation.113 | convolution fusion | flops 402655232 | bytes 6291584 | tf_op jit(solution)/shard_map/dot_general | solution.py:142
  189.6 41.8 %all-gather.3.cloned.1.call-done = f32[16384,144]{1,0:T(8,128)} async-done(((f32[32,144]{1,0:T(8,128)}), f32[16384,144]{1,0:T(8,128)}) %all-gather.3.cloned.1.call-update) | async-done | bytes 9437200 | tf_op jit(solution)/shard_map/all_gather | solution.py:145
  231.4 7.0 %reduce_sum.9 = f32[32,144]{1,0:T(8,128)S(1)} reduce(f32[512,32,144]{2,1,0:T(8,128)} %bitcast.179, f32[]{:T(128)} %constant.93.clone.1), dimensions={0}, to_apply=%region_5.6 | reduce | flops 2354688 | bytes 9455620 | tf_op jit(solution)/shard_map/reduce_sum | solution.py:145
  239.0 99.2 %reduce-scatter.2.cloned.1.call-done = f32[64,256]{1,0:T(8,128)} async-done(((f32[64,16384]{1,0:T(8,128)}), f32[64,256]{1,0:T(8,128)}) %reduce-scatter.2.cloned.1.call-update) | async-done | bytes 65552 | tf_op jit(solution)/shard_map/reduce_scatter | solution.py:143
  (82 shorter events, 15.6 us)
Async XLA Ops:
  8.0 21.3 %copy-start = (bf16[64,16384]{1,0:T(8,128)(2,1)S(1)}, bf16[64,16384]{1,0:T(8,128)(2,1)}, u32[]{:S(2)}) copy-start(bf16[64,16384]{1,0:T(8,128)(2,1)} %param.11) | copy-start | bytes 6291460
  10.6 17.9 %all-to-all-start = ((s32[8,1,4]{2,1,0:T(1,128)}), s32[8,1,4]{2,1,0:T(1,128)S(1)}, u32[]{:S(2)}, u32[]{:S(2)}) async-start(s32[8,1,4]{2,1,0:T(1,128)} %bitcast.12), calls=%async_computation | async-start | bytes 8192 | tf_op jit(solution)/shard_map/all_to_all | solution.py:119
  32.0 6.4 %copy-start.4 = (s32[1,32]{1,0:T(1,128)S(1)}, s32[1,32]{1,0:T(1,128)}, u32[]{:S(2)}) copy-start(s32[1,32]{1,0:T(1,128)} %param.13) | copy-start | bytes 388
  32.0 7.2 %copy-start.1 = (f32[1,2,4096]{2,1,0:T(2,128)S(1)}, f32[1,2,4096]{2,1,0:T(2,128)}, u32[]{:S(2)}) copy-start(f32[1,2,4096]{2,1,0:T(2,128)} %param.15) | copy-start | bytes 98308
  34.7 31.1 %all-to-all-start.1 = ((bf16[8,4,16384]{2,1,0:T(4,128)(2,1)}), bf16[8,4,16384]{2,1,0:T(4,128)(2,1)S(1)}, u32[]{:S(2)}, u32[]{:S(2)}) async-start(bf16[8,4,16384]{2,1,0:T(4,128)(2,1)} %broadcast_select_fusion), calls=%async_computation.1 | async-start | bytes 2097152 | tf_op jit(solution)/shard_map/all_to_all | solution.py:123
  38.3 193.1 %all-gather.3.cloned.1.call-start = ((), (), s32[]{:S(2)}) async-start(), calls=%async_computation.5 | async-start | bytes 16809984 | tf_op jit(solution)/shard_map/all_gather | solution.py:145
  83.4 0.9 copy-start.2
  83.4 1.0 copy-start.3
  118.4 62.8 %all-to-all-start.2 = ((f32[8,4,16384]{2,1,0:T(4,128)}), f32[8,4,16384]{2,1,0:T(4,128)}, u32[]{:S(2)}, u32[]{:S(2)}) async-start(f32[8,4,16384]{2,1,0:T(4,128)} %reshape_reshape.3), calls=%async_computation.2 | async-start | bytes 4194304 | tf_op jit(solution)/shard_map/all_to_all | solution.py:132
  122.8 215.4 %reduce-scatter.2.cloned.1.call-start = ((), (), s32[]{:S(2)}) async-start(), calls=%async_computation.4 | async-start | bytes 4259840 | tf_op jit(solution)/shard_map/reduce_scatter | solution.py:143
Sparse Core Ops, SparseCore 0:
  86.7 144.5 all-gather.2
Sparse Core Ops, SparseCore 1:
  189.7 148.4 reduce-scatter.1
